TPU v7x, 32 devices: a whole 2x2x4 slice. The times are simulated.
32 devices in a mesh: dp: 4 (over y, x), expert: 8 (over z, core).
Axes of the slice: x: 2, y: 2, z: 4, core: 2. Of those that a mesh axis runs over, the one named last changes fastest.
Arguments:
- tokens: bfloat16 [4096, 3584], P(('dp', 'expert')), may hold values from -6 to 6
- gate_probs: float32 [4096, 8], P(('dp', 'expert')), may hold values from 0.1 to 1
- expert_ids: int32 [4096, 8], P(('dp', 'expert')), may hold values from 0 to 63, all different within a row; in each aligned block of 128 rows (0 to 127, 128 to 255, ...) at most 24 rows name the same one
- cotangent: bfloat16 [4096, 3584], P(('dp', 'expert')), may hold values from -6 to 6
- w_gate: bfloat16 [8, 3584, 2048], P('expert', None, 'dp'), may hold values from -0.09375 to 0.09375
- w_up: bfloat16 [8, 3584, 2048], P('expert', None, 'dp'), may hold values from -0.09375 to 0.09375
- w_down: bfloat16 [8, 2048, 3584], P('expert', 'dp'), may hold values from -0.125 to 0.125
Outputs:
- layer_out: bfloat16 [4096, 3584], P(('dp', 'expert'))
- grad_tokens: bfloat16 [4096, 3584], P(('dp', 'expert'))
- grad_probs: float32 [4096, 8], P(('dp', 'expert'))
- grad_gate: bfloat16 [8, 3584, 2048], P('expert', None, 'dp')
- grad_up: bfloat16 [8, 3584, 2048], P('expert', None, 'dp')
- grad_down: bfloat16 [8, 2048, 3584], P('expert', 'dp')
Inputs may be any that keep to these rules, and one draw needn't show every extreme that they name: `expert_ids`: each token names 8 distinct ids. Among the 128 tokens of one device no id is named by more than 24 of them, a bound that some block reaches. Only ids below 8 belong to the window.
All inputs are finite; a program needn't handle non-finite values.
Results may differ from a plain program's by a relative error of at most 0.012.
Values may be sent and summed in bfloat16 or wider, within the bound.
No kernel may reach another device: no remote copies, remote signals or barrier semaphores. Data moves between devices by JAX's collectives and lax.ppermute only.
A program may use at most 192 MiB of HBM per device.

v0:
```python
import jax
import jax.numpy as jnp
from jax import lax
from jax.sharding import PartitionSpec as P


def slot_table(flat_ids, experts, capacity, sentinel):
    matches = (flat_ids[:, None] == jnp.arange(experts, dtype=jnp.int32)[None, :]).astype(jnp.int32)
    earlier = jnp.cumsum(matches, axis=0) - matches
    slot_pos = jnp.sum(earlier * matches, axis=1)
    target = jnp.where(flat_ids < experts, flat_ids * capacity + slot_pos, experts * capacity)
    flat_index = jnp.arange(flat_ids.shape[0], dtype=jnp.int32)
    blank_table = jnp.full((experts * capacity,), sentinel, jnp.int32)
    return blank_table.at[target].set(flat_index, mode="drop")


def contract_last(left, right):
    return lax.dot_general(
        left, right, (((1,), (1,)), ((), ())), preferred_element_type=jnp.float32
    )


def contract_first(left, right):
    return lax.dot_general(
        left, right, (((0,), (0,)), ((), ())), preferred_element_type=jnp.float32
    )


def dispatch(send_rows):
    along_expert = lax.all_to_all(send_rows, "expert", split_axis=0, concat_axis=0, tiled=True)
    return lax.all_gather(along_expert, "dp", axis=0, tiled=True)


def gather_back(partial_rows, groups):
    summed = lax.psum_scatter(partial_rows, "dp", scatter_dimension=0, tiled=True)
    return lax.all_to_all(summed, "expert", split_axis=0, concat_axis=0, tiled=True)


def expert_forward(rows_x, gate_w, up_w, down_w):
    gate_pre = jnp.dot(rows_x, gate_w, preferred_element_type=jnp.float32)
    up_pre = jnp.dot(rows_x, up_w, preferred_element_type=jnp.float32)
    hidden = (gate_pre * jax.nn.sigmoid(gate_pre) * up_pre).astype(jnp.bfloat16)
    part_out = jnp.dot(hidden, down_w, preferred_element_type=jnp.float32).astype(jnp.bfloat16)
    return lax.optimization_barrier((part_out, hidden, gate_pre, up_pre))


def expert_backward(rows_c, gate_pre, up_pre, gate_w, up_w, down_w):
    sigmoid_g = jax.nn.sigmoid(gate_pre)
    activated = gate_pre * sigmoid_g
    grad_hidden = contract_last(rows_c, down_w)
    grad_upin = (grad_hidden * activated).astype(jnp.bfloat16)
    grad_gatein = (grad_hidden * up_pre * sigmoid_g * (1.0 + gate_pre * (1.0 - sigmoid_g))).astype(
        jnp.bfloat16
    )
    part_dx = (contract_last(grad_gatein, gate_w) + contract_last(grad_upin, up_w)).astype(
        jnp.bfloat16
    )
    return (part_dx, grad_gatein, grad_upin)


def join_slots(chunks, experts, model_width):
    parts = [chunk.reshape(experts, -1, model_width) for chunk in chunks]
    return jnp.concatenate(parts, axis=1).reshape(-1, model_width)


def on_device(tokens, gate_probs, expert_ids, cotangent, w_gate, w_up, w_down):
    tok_count, model_width = tokens.shape
    top_k = expert_ids.shape[1]
    experts = lax.axis_size("expert")
    groups = lax.axis_size("dp")
    capacity = 3 * tok_count * top_k // (16 * experts)
    flat_count = tok_count * top_k
    slots = slot_table(expert_ids.reshape(-1), experts, capacity, flat_count)
    token_of = slots // top_k
    zero_row = jnp.zeros((1, model_width), jnp.bfloat16)
    send_x = jnp.concatenate([tokens, zero_row], 0)[token_of]
    rows_dy = jnp.concatenate([cotangent, zero_row], 0)[token_of]
    prob_rows = jnp.concatenate([gate_probs.reshape(-1), jnp.zeros((1,), jnp.float32)], 0)[slots]
    send_c = (prob_rows[:, None] * rows_dy.astype(jnp.float32)).astype(jnp.bfloat16)
    half = max(capacity // 2, 1)
    bounds = [(lo, hi) for lo, hi in ((0, half), (half, capacity)) if hi > lo]
    x_by_slot = send_x.reshape(experts, capacity, model_width)
    c_by_slot = send_c.reshape(experts, capacity, model_width)
    xs = [dispatch(x_by_slot[:, lo:hi].reshape(-1, model_width)) for lo, hi in bounds]
    cs = [dispatch(c_by_slot[:, lo:hi].reshape(-1, model_width)) for lo, hi in bounds]
    gate_w = w_gate[0]
    up_w = w_up[0]
    down_w = w_down[0]
    forwards = [expert_forward(rows_x, gate_w, up_w, down_w) for rows_x in xs]
    outs = [gather_back(fw[0], groups) for fw in forwards]
    backwards = [
        expert_backward(rows_c, fw[2], fw[3], gate_w, up_w, down_w)
        for rows_c, fw in zip(cs, forwards)
    ]
    dxs = [gather_back(bw[0], groups) for bw in backwards]
    new_gate = sum((contract_first(rx, bw[1]) for rx, bw in zip(xs, backwards)))
    new_up = sum((contract_first(rx, bw[2]) for rx, bw in zip(xs, backwards)))
    new_down = sum((contract_first(fw[1], rc) for fw, rc in zip(forwards, cs)))
    new_gate = new_gate.astype(jnp.bfloat16)[None]
    new_up = new_up.astype(jnp.bfloat16)[None]
    new_down = new_down.astype(jnp.bfloat16)[None]
    out_rows = join_slots(outs, experts, model_width).astype(jnp.float32)
    dx_rows = join_slots(dxs, experts, model_width).astype(jnp.float32)
    owner = (token_of[None, :] == jnp.arange(tok_count, dtype=jnp.int32)[:, None]).astype(
        jnp.float32
    )
    layer_out = jnp.dot(
        owner * prob_rows[None, :],
        out_rows,
        precision=lax.Precision.HIGHEST,
        preferred_element_type=jnp.float32,
    ).astype(jnp.bfloat16)
    grad_tokens = jnp.dot(
        owner, dx_rows, precision=lax.Precision.HIGHEST, preferred_element_type=jnp.float32
    ).astype(jnp.bfloat16)
    score_rows = jnp.sum(rows_dy.astype(jnp.float32) * out_rows, axis=1)
    grad_probs = (
        jnp.zeros((flat_count + 1,), jnp.float32)
        .at[slots]
        .set(score_rows)[:flat_count]
        .reshape(tok_count, top_k)
    )
    return (layer_out, grad_tokens, grad_probs, new_gate, new_up, new_down)


def solution(mesh):
    return jax.shard_map(
        on_device,
        mesh=mesh,
        in_specs=(
            P(("dp", "expert"), None),
            P(("dp", "expert"), None),
            P(("dp", "expert"), None),
            P(("dp", "expert"), None),
            P("expert", None, "dp"),
            P("expert", None, "dp"),
            P("expert", "dp", None),
        ),
        out_specs=(
            P(("dp", "expert"), None),
            P(("dp", "expert"), None),
            P(("dp", "expert"), None),
            P("expert", None, "dp"),
            P("expert", None, "dp"),
            P("expert", "dp", None),
        ),
        check_vma=False,
    )
```

profile of v0, /device:TPU:0, one launch (start us, length us, event | category | flops | bytes accessed | tf_op | source)
XLA Modules:
  0.0 435.6 jit_solution(945280252774466416)
XLA Ops:
  12.9 4.3 scatter_custom_fusion
  20.1 29.9 %all_to_all.72 = bf16[8,12,3584]{2,1,0:T(8,128)(2,1)S(1)} all-to-all(bf16[8,12,3584]{2,1,0:T(8,128)(2,1)S(1)} %get-tuple-element.37), channel_id=1, replica_groups=mesh['dp'=4,'expert'=8] {'expert'}, dimensions={0} | all-to-all | bytes 1376256 | tf_op jit(solution)/shard_map/all_to_all | solution.py:30
  51.1 26.3 %all_to_all.73 = bf16[8,12,3584]{2,1,0:T(8,128)(2,1)S(1)} all-to-all(bf16[8,12,3584]{2,1,0:T(8,128)(2,1)S(1)} %get-tuple-element.36), channel_id=1, replica_groups=mesh['dp'=4,'expert'=8] {'expert'}, dimensions={0} | all-to-all | bytes 1376256 | tf_op jit(solution)/shard_map/all_to_all | solution.py:30
  82.9 26.2 %all_to_all.74 = bf16[8,12,3584]{2,1,0:T(8,128)(2,1)S(1)} all-to-all(bf16[8,12,3584]{2,1,0:T(8,128)(2,1)S(1)} %get-tuple-element.34), channel_id=1, replica_groups=mesh['dp'=4,'expert'=8] {'expert'}, dimensions={0} | all-to-all | bytes 1376256 | tf_op jit(solution)/shard_map/all_to_all | solution.py:30
  110.1 26.2 %all_to_all.75 = bf16[8,12,3584]{2,1,0:T(8,128)(2,1)S(1)} all-to-all(bf16[8,12,3584]{2,1,0:T(8,128)(2,1)S(1)} %get-tuple-element.35), channel_id=1, replica_groups=mesh['dp'=4,'expert'=8] {'expert'}, dimensions={0} | all-to-all | bytes 1376256 | tf_op jit(solution)/shard_map/all_to_all | solution.py:30
  137.4 4.6 %fusion.21 = f32[384,512]{1,0:T(8,128)S(1)} fusion(bf16[384,3584]{1,0:T(8,128)(2,1)} %all-gather.7.cloned.1.call-done, bf16[1,3584,512]{2,1,0:T(8,128)(2,1)} %param.11), kind=kOutput, calls=%fused_computation.35 | convolution fusion | flops 1409286144 | bytes 7208960 | tf_op jit(solution)/shard_map/dot_general | solution.py:40
  148.9 4.6 %fusion.23 = f32[384,512]{1,0:T(8,128)S(1)} fusion(bf16[384,3584]{1,0:T(8,128)(2,1)} %all-gather.5.cloned.1.call-done, bf16[1,3584,512]{2,1,0:T(8,128)(2,1)} %param.11), kind=kOutput, calls=%fused_computation.37 | convolution fusion | flops 1409286144 | bytes 7208960 | tf_op jit(solution)/shard_map/dot_general | solution.py:40
  160.1 16.6 %all-gather.9.cloned.1.call-done = bf16[384,3584]{1,0:T(8,128)(2,1)} async-done(((bf16[96,3584]{1,0:T(8,128)(2,1)}), bf16[384,3584]{1,0:T(8,128)(2,1)}) %all-gather.9.cloned.1.call-update) | async-done | bytes 2752528 | tf_op jit(solution)/shard_map/all_gather | solution.py:31
  176.7 5.2 %multiply_convert_fusion.3 = (bf16[384,512]{1,0:T(8,128)(2,1)S(1)}, bf16[384,512]{1,0:T(8,128)(2,1)S(1)}) fusion(f32[384,512]{1,0:T(8,128)} %copy-done.24, f32[384,512]{1,0:T(8,128)} %get-tuple-element.16, bf16[384,3584]{1,0:T(8,128)(2,1)} %all-gather.9.cloned.1.call-done, bf16[1,512,3584]{2,1,0:T(8,128)(2,1)} %param.13), kind=kOutput, calls=%fused_computation.46 | convolution fusion | flops 1411842048 | bytes 8781824 | tf_op jit(solution)/shard_map/dot_general | solution.py:18
  187.2 32.0 %all-gather.11.cloned.1.call-done = bf16[384,3584]{1,0:T(8,128)(2,1)} async-done(((bf16[96,3584]{1,0:T(8,128)(2,1)}), bf16[384,3584]{1,0:T(8,128)(2,1)}) %all-gather.11.cloned.1.call-update) | async-done | bytes 2752528 | tf_op jit(solution)/shard_map/all_gather | solution.py:31
  219.1 5.2 %multiply_convert_fusion.1 = (bf16[384,512]{1,0:T(8,128)(2,1)S(1)}, bf16[384,512]{1,0:T(8,128)(2,1)S(1)}) fusion(f32[384,512]{1,0:T(8,128)} %copy-done.23, f32[384,512]{1,0:T(8,128)} %get-tuple-element.18, bf16[384,3584]{1,0:T(8,128)(2,1)} %all-gather.11.cloned.1.call-done, bf16[1,512,3584]{2,1,0:T(8,128)(2,1)} %param.13), kind=kOutput, calls=%fused_computation.43 | convolution fusion | flops 1411842048 | bytes 8781824 | tf_op jit(solution)/shard_map/dot_general | solution.py:18
  229.9 33.3 %reduce-scatter.7.cloned.1.call-done = bf16[96,3584]{1,0:T(8,128)(2,1)} async-done(((bf16[384,3584]{1,0:T(8,128)(2,1)}), bf16[96,3584]{1,0:T(8,128)(2,1)}) %reduce-scatter.7.cloned.1.call-update) | async-done | bytes 688144 | tf_op jit(solution)/shard_map/reduce_scatter | solution.py:35
  265.4 4.6 %all-to-all-start.3 = ((bf16[8,12,3584]{2,1,0:T(8,128)(2,1)}), bf16[8,12,3584]{2,1,0:T(8,128)(2,1)}, u32[]{:S(2)}, u32[]{:S(2)}) async-start(bf16[8,12,3584]{2,1,0:T(8,128)(2,1)} %all_to_all.54), calls=%async_computation.5 | async-start | bytes 1835008 | tf_op jit(solution)/shard_map/all_to_all | solution.py:36
  270.0 37.5 %reduce-scatter.5.cloned.1.call-done = bf16[96,3584]{1,0:T(8,128)(2,1)} async-done(((bf16[384,3584]{1,0:T(8,128)(2,1)}), bf16[96,3584]{1,0:T(8,128)(2,1)}) %reduce-scatter.5.cloned.1.call-update) | async-done | bytes 688144 | tf_op jit(solution)/shard_map/reduce_scatter | solution.py:35
  309.5 4.6 %all-to-all-start.1 = ((bf16[8,12,3584]{2,1,0:T(8,128)(2,1)}), bf16[8,12,3584]{2,1,0:T(8,128)(2,1)}, u32[]{:S(2)}, u32[]{:S(2)}) async-start(bf16[8,12,3584]{2,1,0:T(8,128)(2,1)} %all_to_all.50), calls=%async_computation.2 | async-start | bytes 1835008 | tf_op jit(solution)/shard_map/all_to_all | solution.py:36
  318.1 4.1 fusion.3
  322.1 29.6 %reduce-scatter.9.cloned.1.call-done = bf16[96,3584]{1,0:T(8,128)(2,1)} async-done(((bf16[384,3584]{1,0:T(8,128)(2,1)}), bf16[96,3584]{1,0:T(8,128)(2,1)}) %reduce-scatter.9.cloned.1.call-update) | async-done | bytes 688144 | tf_op jit(solution)/shard_map/reduce_scatter | solution.py:35
  353.8 4.6 %all-to-all-start.5 = ((bf16[8,12,3584]{2,1,0:T(8,128)(2,1)}), bf16[8,12,3584]{2,1,0:T(8,128)(2,1)}, u32[]{:S(2)}, u32[]{:S(2)}) async-start(bf16[8,12,3584]{2,1,0:T(8,128)(2,1)} %all_to_all.58), calls=%async_computation.8 | async-start | bytes 1835008 | tf_op jit(solution)/shard_map/all_to_all | solution.py:36
  362.5 5.0 %fusion.43 = f32[512,3584]{1,0:T(8,128)} fusion(bf16[384,512]{1,0:T(8,128)(2,1)S(1)} %copy-done.19, bf16[384,3584]{1,0:T(8,128)(2,1)S(1)} %copy-done.10), kind=kOutput, calls=%fused_computation.87 | convolution fusion | flops 1409286144 | bytes 10485760 | tf_op jit(solution)/shard_map/dot_general | solution.py:24
  367.5 4.1 fusion.2
  371.5 23.9 %reduce-scatter.11.cloned.1.call-done = bf16[96,3584]{1,0:T(8,128)(2,1)} async-done(((bf16[384,3584]{1,0:T(8,128)(2,1)}), bf16[96,3584]{1,0:T(8,128)(2,1)}) %reduce-scatter.11.cloned.1.call-update) | async-done | bytes 688144 | tf_op jit(solution)/shard_map/reduce_scatter | solution.py:35
  397.5 4.6 %all-to-all-start.7 = ((bf16[8,12,3584]{2,1,0:T(8,128)(2,1)}), bf16[8,12,3584]{2,1,0:T(8,128)(2,1)S(1)}, u32[]{:S(2)}, u32[]{:S(2)}) async-start(bf16[8,12,3584]{2,1,0:T(8,128)(2,1)} %all_to_all.62), calls=%async_computation.11 | async-start | bytes 1835008 | tf_op jit(solution)/shard_map/all_to_all | solution.py:36
  402.1 7.9 %fusion.4 = bf16[1,512,3584]{2,1,0:T(8,128)(2,1)} fusion(f32[512,3584]{1,0:T(8,128)} %fusion.43, bf16[384,512]{1,0:T(8,128)(2,1)S(1)} %copy-done.17, bf16[384,3584]{1,0:T(8,128)(2,1)} %all-gather.11.cloned.1.call-done), kind=kOutput, calls=%fused_computation.16 | convolution fusion | flops 1412956160 | bytes 14155776 | tf_op jit(solution)/shard_map/dot_general | solution.py:24
  416.1 9.8 %all-to-all-done.7 = bf16[8,12,3584]{2,1,0:T(8,128)(2,1)S(1)} async-done(((bf16[8,12,3584]{2,1,0:T(8,128)(2,1)}), bf16[8,12,3584]{2,1,0:T(8,128)(2,1)S(1)}, u32[]{:S(2)}, u32[]{:S(2)}) %all-to-all-start.7) | async-done | bytes 688160 | tf_op jit(solution)/shard_map/all_to_all | solution.py:36
  (130 shorter events, 66.5 us)
Async XLA Ops:
  7.2 130.3 %all-gather.7.cloned.1.call-start = ((), (), s32[]{:S(2)}) async-start(), calls=%async_computation.14 | async-start | bytes 3440640 | tf_op jit(solution)/shard_map/all_gather | solution.py:31
  51.0 27.5 %copy-start.20 = (f32[128,8]{0,1:T(8,128)S(1)}, f32[128,8]{0,1:T(8,128)}, u32[]{:S(2)}) copy-start(f32[128,8]{0,1:T(8,128)} %param.8) | copy-start | bytes 12292
  51.1 29.2 %copy-start.15 = (bf16[128,3584]{1,0:T(8,128)(2,1)S(1)}, bf16[128,3584]{1,0:T(8,128)(2,1)}, u32[]{:S(2)}) copy-start(bf16[128,3584]{1,0:T(8,128)(2,1)} %param.10) | copy-start | bytes 2752516
  51.1 97.8 %all-gather.5.cloned.1.call-start = ((), (), s32[]{:S(2)}) async-start(), calls=%async_computation.12 | async-start | bytes 3440640 | tf_op jit(solution)/shard_map/all_gather | solution.py:31
  78.5 98.2 %all-gather.9.cloned.1.call-start = ((), (), s32[]{:S(2)}) async-start(), calls=%async_computation.16 | async-start | bytes 3440640 | tf_op jit(solution)/shard_map/all_gather | solution.py:31
  110.1 109.0 %all-gather.11.cloned.1.call-start = ((), (), s32[]{:S(2)}) async-start(), calls=%async_computation.18 | async-start | bytes 3440640 | tf_op jit(solution)/shard_map/all_gather | solution.py:31
  137.4 125.9 %reduce-scatter.7.cloned.1.call-start = ((), (), s32[]{:S(2)}) async-start(), calls=%async_computation.15 | async-start | bytes 3440640 | tf_op jit(solution)/shard_map/reduce_scatter | solution.py:35
  137.4 4.6 %copy-start = (bf16[384,3584]{1,0:T(8,128)(2,1)S(1)}, bf16[384,3584]{1,0:T(8,128)(2,1)}, u32[]{:S(2)}) copy-start(bf16[384,3584]{1,0:T(8,128)(2,1)} %all-gather.7.cloned.1.call-done) | copy-start | bytes 8257540
  137.4 4.8 %copy-start.3 = (bf16[1,3584,512]{2,1,0:T(8,128)(2,1)S(1)}, bf16[1,3584,512]{2,1,0:T(8,128)(2,1)}, u32[]{:S(2)}) copy-start(bf16[1,3584,512]{2,1,0:T(8,128)(2,1)} %param.12) | copy-start | bytes 11010052
  148.6 158.8 %reduce-scatter.5.cloned.1.call-start = ((), (), s32[]{:S(2)}) async-start(), calls=%async_computation.13 | async-start | bytes 3440640 | tf_op jit(solution)/shard_map/reduce_scatter | solution.py:35
  148.8 4.6 %copy-start.4 = (bf16[1,3584,512]{2,1,0:T(8,128)(2,1)S(1)}, bf16[1,3584,512]{2,1,0:T(8,128)(2,1)}, u32[]{:S(2)}) copy-start(bf16[1,3584,512]{2,1,0:T(8,128)(2,1)} %param.12) | copy-start | bytes 11010052
  148.9 4.8 %copy-start.7 = (bf16[384,3584]{1,0:T(8,128)(2,1)S(1)}, bf16[384,3584]{1,0:T(8,128)(2,1)}, u32[]{:S(2)}) copy-start(bf16[384,3584]{1,0:T(8,128)(2,1)} %all-gather.5.cloned.1.call-done) | copy-start | bytes 8257540
  160.0 191.7 %reduce-scatter.9.cloned.1.call-start = ((), (), s32[]{:S(2)}) async-start(), calls=%async_computation.17 | async-start | bytes 3440640 | tf_op jit(solution)/shard_map/reduce_scatter | solution.py:35
  176.7 5.2 %copy-start.1 = (bf16[1,3584,512]{2,1,0:T(8,128)(2,1)S(1)}, bf16[1,3584,512]{2,1,0:T(8,128)(2,1)}, u32[]{:S(2)}) copy-start(bf16[1,3584,512]{2,1,0:T(8,128)(2,1)} %param.11) | copy-start | bytes 11010052
  187.1 208.3 %reduce-scatter.11.cloned.1.call-start = ((), (), s32[]{:S(2)}) async-start(), calls=%async_computation.19 | async-start | bytes 3440640 | tf_op jit(solution)/shard_map/reduce_scatter | solution.py:35
  219.1 5.2 %copy-start.2 = (bf16[1,3584,512]{2,1,0:T(8,128)(2,1)S(1)}, bf16[1,3584,512]{2,1,0:T(8,128)(2,1)}, u32[]{:S(2)}) copy-start(bf16[1,3584,512]{2,1,0:T(8,128)(2,1)} %param.11) | copy-start | bytes 11010052
  265.4 44.1 %all-to-all-start.3 = ((bf16[8,12,3584]{2,1,0:T(8,128)(2,1)}), bf16[8,12,3584]{2,1,0:T(8,128)(2,1)}, u32[]{:S(2)}, u32[]{:S(2)}) async-start(bf16[8,12,3584]{2,1,0:T(8,128)(2,1)} %all_to_all.54), calls=%async_computation.5 | async-start | bytes 1835008 | tf_op jit(solution)/shard_map/all_to_all | solution.py:36
  309.5 44.3 %all-to-all-start.1 = ((bf16[8,12,3584]{2,1,0:T(8,128)(2,1)}), bf16[8,12,3584]{2,1,0:T(8,128)(2,1)}, u32[]{:S(2)}, u32[]{:S(2)}) async-start(bf16[8,12,3584]{2,1,0:T(8,128)(2,1)} %all_to_all.50), calls=%async_computation.2 | async-start | bytes 1835008 | tf_op jit(solution)/shard_map/all_to_all | solution.py:36
  353.8 43.7 %all-to-all-start.5 = ((bf16[8,12,3584]{2,1,0:T(8,128)(2,1)}), bf16[8,12,3584]{2,1,0:T(8,128)(2,1)}, u32[]{:S(2)}, u32[]{:S(2)}) async-start(bf16[8,12,3584]{2,1,0:T(8,128)(2,1)} %all_to_all.58), calls=%async_computation.8 | async-start | bytes 1835008 | tf_op jit(solution)/shard_map/all_to_all | solution.py:36
  358.4 4.0 copy-start.10
  358.4 4.1 copy-start.19
  362.4 5.0 %copy-start.12 = (bf16[384,512]{1,0:T(8,128)(2,1)S(1)}, bf16[384,512]{1,0:T(8,128)(2,1)}, u32[]{:S(2)}) copy-start(bf16[384,512]{1,0:T(8,128)(2,1)} %copy-done.11) | copy-start | bytes 1179652
  371.5 30.5 %copy-start.17 = (bf16[384,512]{1,0:T(8,128)(2,1)S(1)}, bf16[384,512]{1,0:T(8,128)(2,1)}, u32[]{:S(2)}) copy-start(bf16[384,512]{1,0:T(8,128)(2,1)} %copy-done.16) | copy-start | bytes 1179652
  397.5 28.4 %all-to-all-start.7 = ((bf16[8,12,3584]{2,1,0:T(8,128)(2,1)}), bf16[8,12,3584]{2,1,0:T(8,128)(2,1)S(1)}, u32[]{:S(2)}, u32[]{:S(2)}) async-start(bf16[8,12,3584]{2,1,0:T(8,128)(2,1)} %all_to_all.62), calls=%async_computation.11 | async-start | bytes 1835008 | tf_op jit(solution)/shard_map/all_to_all | solution.py:36
  (13 other events, 27.5 us)
Sparse Core Ops, SparseCore 0:
  51.2 39.6 all-gather.6
  93.3 40.7 all-gather.4
  135.9 40.7 all-gather.8
  178.4 40.7 all-gather.10
  222.6 40.6 reduce-scatter.6
  266.7 40.6 reduce-scatter.4
  311.0 40.6 reduce-scatter.8
  354.7 40.6 reduce-scatter.10
where the time goes:
time: 436 us
  waiting for transfers between devices  183 us (42%)
  blocking collectives  109 us (25%)
  matrix products  72.5 us (17%)
  local copies, waits for them, and re-layouts  30.1 us (7%)
  starting transfers between devices  18.9 us (4%)
  between operations  14.6 us (3%)
  other arithmetic  8.13 us (2%)
    reduce_scatter x4, waiting for transfers between devices, gather_back(): lax.psum_scatter(partial_rows, 'dp', scatter_dimension=0, tiled=True)  124 us
    all_to_all x4, blocking collectives, dispatch(): lax.all_to_all(send_rows, 'expert', split_axis=0, concat_axis=0, tiled=True)  109 us
    all_gather x4, waiting for transfers between devices, dispatch(): return lax.all_gather(along_expert, 'dp', axis=0, tiled=True)  48.6 us
    dot_general x6, matrix products, contract_first(): lax.dot_general(left, right, (((0,), (0,)), ((), ())), preferred_element_...  29 us
    dot_general x6, matrix products, contract_last(): lax.dot_general(left, right, (((1,), (1,)), ((), ())), preferred_element_...  20 us
    all_to_all x4, starting transfers between devices, gather_back(): lax.all_to_all(summed, 'expert', split_axis=0, concat_axis=0, tiled=True)  18.4 us
    all_to_all x4, waiting for transfers between devices, gather_back(): lax.all_to_all(summed, 'expert', split_axis=0, concat_axis=0, tiled=True)  9.8 us
    dot_general x2, matrix products, expert_forward(): gate_pre = jnp.dot(rows_x, gate_w, preferred_element_type=jnp.float32)  9.19 us
  transfers between devices with their start and end apart: 12, of which 7 were waited for; matrix products, arithmetic and copies ran while one was open for 18% of the time, Pallas kernels for 0%

commit v1 on v0

--- a/solution.py
+++ b/solution.py
@@ -2,6 +2,18 @@
 import jax.numpy as jnp
 from jax import lax
 from jax.sharding import PartitionSpec as P
+
+
+def doubled_up(x, axis, dim):
+    ways, here = (lax.axis_size(axis), lax.axis_index(axis))
+    grown, reach = (x, 1)
+    while reach < ways:
+        theirs = lax.ppermute(grown, axis, [(d, d ^ reach) for d in range(ways)])
+        mine_first = jnp.concatenate([grown, theirs], axis=dim)
+        theirs_first = jnp.concatenate([theirs, grown], axis=dim)
+        grown = jnp.where(here & reach == 0, mine_first, theirs_first)
+        reach = 2 * reach
+    return grown
 
 
 def slot_table(flat_ids, experts, capacity, sentinel):
@@ -28,7 +40,7 @@
 
 def dispatch(send_rows):
     along_expert = lax.all_to_all(send_rows, "expert", split_axis=0, concat_axis=0, tiled=True)
-    return lax.all_gather(along_expert, "dp", axis=0, tiled=True)
+    return doubled_up(along_expert, "dp", 0)
 
 
 def gather_back(partial_rows, groups):

time: 436 us -> 461 us (1.057); the launches traced: 436 us -> 452 us
  blocking collectives: 109 us -> 29.9 us
  waiting for transfers between devices: 183 us -> 227 us
  matrix products: 72.5 us -> 98.8 us
  starting transfers between devices: 18.9 us -> 43 us
    ppermute x0 -> x8, waiting for transfers between devices: none -> 193 us  [doubled_up(): theirs = lax.ppermute(grown, axis, [(d, d ^ reach) for d in range(ways)])]
    reduce_scatter x4, waiting for transfers between devices: 124 us -> 0.03 us  [gather_back(): lax.psum_scatter(partial_rows, 'dp', scatter_dimension=0, tiled=True)]
    all_to_all x4 -> x1, blocking collectives: 109 us -> 29.9 us  [dispatch(): lax.all_to_all(send_rows, 'expert', split_axis=0, concat_axis=0, tiled=True)]
    all_gather x4 -> x0, waiting for transfers between devices: 48.6 us -> none  [dispatch(): return lax.all_gather(along_expert, 'dp', axis=0, tiled=True)]
    all_to_all x4, waiting for transfers between devices: 9.8 us -> 34.2 us  [gather_back(): lax.all_to_all(summed, 'expert', split_axis=0, concat_axis=0, tiled=True)]
    dot_general x6, matrix products: 29 us -> 49.7 us  [contract_first(): lax.dot_general(left, right, (((0,), (0,)), ((), ())), preferred_element_...]
    all_to_all x0 -> x3, starting transfers between devices: none -> 12.7 us  [dispatch(): lax.all_to_all(send_rows, 'expert', split_axis=0, concat_axis=0, tiled=True)]
    ppermute x0 -> x8, starting transfers between devices: none -> 8 us  [doubled_up(): theirs = lax.ppermute(grown, axis, [(d, d ^ reach) for d in range(ways)])]
  transfers between devices with their start and end apart: 12 -> 19, of which waited for: 7 -> 12; matrix products, arithmetic and copies ran while one was open for 18% -> 24% of each run, Pallas kernels for 0% -> 0%
where the time goes in v1:
time: 461 us; the launch traced here: 452 us
  waiting for transfers between devices  227 us (49%)
  matrix products  98.8 us (21%)
  starting transfers between devices  43 us (9%)
  blocking collectives  29.9 us (6%)
  local copies, waits for them, and re-layouts  28 us (6%)
  between operations  14.6 us (3%)
  other arithmetic  11.3 us (2%)
    ppermute x8, waiting for transfers between devices, doubled_up(): theirs = lax.ppermute(grown, axis, [(d, d ^ reach) for d in range(ways)])  193 us
    dot_general x6, matrix products, contract_first(): lax.dot_general(left, right, (((0,), (0,)), ((), ())), preferred_element_...  49.7 us
    all_to_all x4, waiting for transfers between devices, gather_back(): lax.all_to_all(summed, 'expert', split_axis=0, concat_axis=0, tiled=True)  34.2 us
    all_to_all x1, blocking collectives, dispatch(): lax.all_to_all(send_rows, 'expert', split_axis=0, concat_axis=0, tiled=True)  29.9 us
    all_to_all x4, starting transfers between devices, gather_back(): lax.all_to_all(summed, 'expert', split_axis=0, concat_axis=0, tiled=True)  21.5 us
    dot_general x6, matrix products, contract_last(): lax.dot_general(left, right, (((1,), (1,)), ((), ())), preferred_element_...  19.9 us
    all_to_all x3, starting transfers between devices, dispatch(): lax.all_to_all(send_rows, 'expert', split_axis=0, concat_axis=0, tiled=True)  12.7 us
    dot_general x2, matrix products, expert_forward(): up_pre = jnp.dot(rows_x, up_w, preferred_element_type=jnp.float32)  9.92 us
  transfers between devices with their start and end apart: 19, of which 12 were waited for; matrix products, arithmetic and copies ran while one was open for 24% of the time, Pallas kernels for 0%

profile of v1, /device:TPU:0, one launch (start us, length us, event | category | flops | bytes accessed | tf_op | source)
XLA Modules:
  0.0 452.5 jit_solution(9521798020421748610)
XLA Ops:
  21.0 29.9 %all_to_all.72 = bf16[8,12,3584]{2,1,0:T(8,128)(2,1)S(1)} all-to-all(bf16[8,12,3584]{2,1,0:T(8,128)(2,1)S(1)} %get-tuple-element.37), channel_id=1, replica_groups=mesh['dp'=4,'expert'=8] {'expert'}, dimensions={0} | all-to-all | bytes 1376256 | tf_op jit(solution)/shard_map/all_to_all | solution.py:42
  52.6 15.5 %collective-permute-done.2 = bf16[96,3584]{1,0:T(8,128)(2,1)S(1)} collective-permute-done((bf16[96,3584]{1,0:T(8,128)(2,1)S(1)}, bf16[96,3584]{1,0:T(8,128)(2,1)S(1)}, u32[]{:S(2)}, u32[]{:S(2)}) %collective-permute-start.2) | collective-permute-done | bytes 688160 | tf_op jit(solution)/shard_map/ppermute | solution.py:11
  73.6 25.8 %collective-permute-done.3 = bf16[192,3584]{1,0:T(8,128)(2,1)} collective-permute-done((bf16[192,3584]{1,0:T(8,128)(2,1)S(1)}, bf16[192,3584]{1,0:T(8,128)(2,1)}, u32[]{:S(2)}, u32[]{:S(2)}) %collective-permute-start.3) | collective-permute-done | bytes 1376288 | tf_op jit(solution)/shard_map/ppermute | solution.py:11
  117.8 19.4 %collective-permute-done = bf16[96,3584]{1,0:T(8,128)(2,1)} collective-permute-done((bf16[96,3584]{1,0:T(8,128)(2,1)S(1)}, bf16[96,3584]{1,0:T(8,128)(2,1)}, u32[]{:S(2)}, u32[]{:S(2)}) %collective-permute-start) | collective-permute-done | bytes 688160 | tf_op jit(solution)/shard_map/ppermute | solution.py:11
  147.2 26.6 %collective-permute-done.1 = bf16[192,3584]{1,0:T(8,128)(2,1)} collective-permute-done((bf16[192,3584]{1,0:T(8,128)(2,1)}, bf16[192,3584]{1,0:T(8,128)(2,1)}, u32[]{:S(2)}, u32[]{:S(2)}) %collective-permute-start.1) | collective-permute-done | bytes 1376288 | tf_op jit(solution)/shard_map/ppermute | solution.py:11
  173.8 5.3 %fusion.23 = f32[384,512]{1,0:T(8,128)S(1)} fusion(bf16[1,3584,512]{2,1,0:T(8,128)(2,1)} %param.11, bf16[192,3584]{1,0:T(8,128)(2,1)} %collective-permute-done.1, bf16[192,3584]{1,0:T(8,128)(2,1)} %maximum_select_fusion.4, pred[]{:T(512)S(6)} %eq.61), kind=kOutput, calls=%fused_computation.37 | convolution fusion | flops 1421672448 | bytes 7208961 | tf_op jit(solution)/shard_map/dot_general | solution.py:52
  179.2 5.4 %multiply_convert_fusion.6 = (bf16[384,512]{1,0:T(8,128)(2,1)S(1)}, f32[384,512]{1,0:T(8,128)}) fusion(f32[384,512]{1,0:T(8,128)S(1)} %fusion.23, bf16[1,3584,512]{2,1,0:T(8,128)(2,1)S(1)} %copy-done.3, bf16[192,3584]{1,0:T(8,128)(2,1)} %collective-permute-done.1, bf16[192,3584]{1,0:T(8,128)(2,1)} %maximum_select_fusion.4, pred[]{:T(512)S(6)} %eq.61), kind=kOutput, calls=%fused_computation.58 | convolution fusion | flops 1422852096 | bytes 8388609 | tf_op jit(solution)/shard_map/dot_general | solution.py:53
  189.3 15.8 %collective-permute-done.4 = bf16[96,3584]{1,0:T(8,128)(2,1)S(1)} collective-permute-done((bf16[96,3584]{1,0:T(8,128)(2,1)S(1)}, bf16[96,3584]{1,0:T(8,128)(2,1)S(1)}, u32[]{:S(2)}, u32[]{:S(2)}) %collective-permute-start.4) | collective-permute-done | bytes 688160 | tf_op jit(solution)/shard_map/ppermute | solution.py:11
  206.4 5.6 %all-to-all-start.6 = ((bf16[8,12,3584]{2,1,0:T(8,128)(2,1)}), bf16[8,12,3584]{2,1,0:T(8,128)(2,1)S(1)}, u32[]{:S(2)}, u32[]{:S(2)}) async-start(bf16[8,12,3584]{2,1,0:T(8,128)(2,1)} %get-tuple-element.35), calls=%async_computation.9 | async-start | bytes 1835008 | tf_op jit(solution)/shard_map/all_to_all | solution.py:42
  212.0 34.8 %collective-permute-done.5 = bf16[192,3584]{1,0:T(8,128)(2,1)} collective-permute-done((bf16[192,3584]{1,0:T(8,128)(2,1)}, bf16[192,3584]{1,0:T(8,128)(2,1)}, u32[]{:S(2)}, u32[]{:S(2)}) %collective-permute-start.5) | collective-permute-done | bytes 1376288 | tf_op jit(solution)/shard_map/ppermute | solution.py:11
  246.8 6.0 %multiply_convert_fusion.3 = (bf16[384,512]{1,0:T(8,128)(2,1)S(1)}, bf16[384,512]{1,0:T(8,128)(2,1)S(1)}) fusion(f32[384,512]{1,0:T(8,128)} %copy-done.27, f32[384,512]{1,0:T(8,128)} %get-tuple-element.16, bf16[1,512,3584]{2,1,0:T(8,128)(2,1)} %param.13, bf16[192,3584]{1,0:T(8,128)(2,1)} %collective-permute-done.5, ...), kind=kOutput, calls=%fused_computation.54 | convolution fusion | flops 1424228352 | bytes 8781825 | tf_op jit(solution)/shard_map/dot_general | solution.py:30
  259.1 13.8 %collective-permute-done.6 = bf16[96,3584]{1,0:T(8,128)(2,1)S(1)} collective-permute-done((bf16[96,3584]{1,0:T(8,128)(2,1)S(1)}, bf16[96,3584]{1,0:T(8,128)(2,1)S(1)}, u32[]{:S(2)}, u32[]{:S(2)}) %collective-permute-start.6) | collective-permute-done | bytes 688160 | tf_op jit(solution)/shard_map/ppermute | solution.py:11
  273.3 41.0 %collective-permute-done.7 = bf16[192,3584]{1,0:T(8,128)(2,1)S(1)} collective-permute-done((bf16[192,3584]{1,0:T(8,128)(2,1)S(1)}, bf16[192,3584]{1,0:T(8,128)(2,1)S(1)}, u32[]{:S(2)}, u32[]{:S(2)}) %collective-permute-start.7) | collective-permute-done | bytes 1376288 | tf_op jit(solution)/shard_map/ppermute | solution.py:11
  326.1 9.9 %all-to-all-start.3 = ((bf16[8,12,3584]{2,1,0:T(8,128)(2,1)}), bf16[8,12,3584]{2,1,0:T(8,128)(2,1)S(1)}, u32[]{:S(2)}, u32[]{:S(2)}) async-start(bf16[8,12,3584]{2,1,0:T(8,128)(2,1)} %all_to_all.54), calls=%async_computation.5 | async-start | bytes 1835008 | tf_op jit(solution)/shard_map/all_to_all | solution.py:48
  336.0 7.7 %fusion.44 = f32[3584,512]{1,0:T(8,128)} fusion(bf16[384,512]{1,0:T(8,128)(2,1)S(1)} %get-tuple-element.32, bf16[192,3584]{1,0:T(8,128)(2,1)} %collective-permute-done.3, bf16[192,3584]{1,0:T(8,128)(2,1)} %copy-done.11, pred[]{:T(512)S(6)} %eq.61), kind=kOutput, calls=%fused_computation.96 | convolution fusion | flops 1421672448 | bytes 10485761 | tf_op jit(solution)/shard_map/dot_general | solution.py:36
  345.9 13.9 %all-to-all-done.3 = bf16[8,12,3584]{2,1,0:T(8,128)(2,1)S(1)} async-done(((bf16[8,12,3584]{2,1,0:T(8,128)(2,1)}), bf16[8,12,3584]{2,1,0:T(8,128)(2,1)S(1)}, u32[]{:S(2)}, u32[]{:S(2)}) %all-to-all-start.3) | async-done | bytes 688160 | tf_op jit(solution)/shard_map/all_to_all | solution.py:48
  363.4 7.9 %fusion.45 = f32[3584,512]{1,0:T(8,128)} fusion(bf16[384,512]{1,0:T(8,128)(2,1)} %copy-done.17, bf16[192,3584]{1,0:T(8,128)(2,1)} %collective-permute-done.3, bf16[192,3584]{1,0:T(8,128)(2,1)} %copy-done.11, pred[]{:T(512)S(6)} %eq.61), kind=kOutput, calls=%fused_computation.97 | convolution fusion | flops 1421672448 | bytes 10485761 | tf_op jit(solution)/shard_map/dot_general | solution.py:36
  371.3 8.8 %fusion.3 = bf16[1,3584,512]{2,1,0:T(8,128)(2,1)} fusion(f32[3584,512]{1,0:T(8,128)} %fusion.44, bf16[384,512]{1,0:T(8,128)(2,1)S(1)} %copy-done.16, bf16[192,3584]{1,0:T(8,128)(2,1)} %collective-permute-done.1, bf16[192,3584]{1,0:T(8,128)(2,1)} %maximum_select_fusion.4, pred[]{:T(512)S(6)} %eq.61), kind=kOutput, calls=%fused_computation.15 | convolution fusion | flops 1425342464 | bytes 14155777 | tf_op jit(solution)/shard_map/dot_general | solution.py:36
  382.2 4.9 %all-to-all-done.1 = bf16[8,12,3584]{2,1,0:T(8,128)(2,1)S(1)} async-done(((bf16[8,12,3584]{2,1,0:T(8,128)(2,1)}), bf16[8,12,3584]{2,1,0:T(8,128)(2,1)S(1)}, u32[]{:S(2)}, u32[]{:S(2)}) %all-to-all-start.1) | async-done | bytes 688160 | tf_op jit(solution)/shard_map/all_to_all | solution.py:48
  390.9 7.8 %fusion.25 = f32[512,3584]{1,0:T(8,128)} fusion(bf16[384,512]{1,0:T(8,128)(2,1)} %copy-done.22, bf16[192,3584]{1,0:T(8,128)(2,1)} %copy-done.21, bf16[192,3584]{1,0:T(8,128)(2,1)} %copy-done.12, pred[]{:T(512)S(6)} %eq.61), kind=kOutput, calls=%fused_computation.59 | convolution fusion | flops 1421672448 | bytes 10485761 | tf_op jit(solution)/shard_map/dot_general | solution.py:36
  398.7 8.7 %fusion.2 = bf16[1,3584,512]{2,1,0:T(8,128)(2,1)} fusion(f32[3584,512]{1,0:T(8,128)} %fusion.45, bf16[384,512]{1,0:T(8,128)(2,1)S(1)} %copy-done.14, bf16[192,3584]{1,0:T(8,128)(2,1)} %collective-permute-done.1, bf16[192,3584]{1,0:T(8,128)(2,1)} %maximum_select_fusion.4, pred[]{:T(512)S(6)} %eq.61), kind=kOutput, calls=%fused_computation.14 | convolution fusion | flops 1425342464 | bytes 14155777 | tf_op jit(solution)/shard_map/dot_general | solution.py:36
  409.6 5.0 %all-to-all-done.5 = bf16[8,12,3584]{2,1,0:T(8,128)(2,1)S(1)} async-done(((bf16[8,12,3584]{2,1,0:T(8,128)(2,1)}), bf16[8,12,3584]{2,1,0:T(8,128)(2,1)S(1)}, u32[]{:S(2)}, u32[]{:S(2)}) %all-to-all-start.5) | async-done | bytes 688160 | tf_op jit(solution)/shard_map/all_to_all | solution.py:48
  418.9 8.8 %fusion.4 = bf16[1,512,3584]{2,1,0:T(8,128)(2,1)} fusion(f32[512,3584]{1,0:T(8,128)} %fusion.25, bf16[384,512]{1,0:T(8,128)(2,1)S(1)} %copy-done.24, bf16[192,3584]{1,0:T(8,128)(2,1)} %collective-permute-done.5, bf16[192,3584]{1,0:T(8,128)(2,1)} %maximum_select_fusion.6, pred[]{:T(512)S(6)} %eq.61), kind=kOutput, calls=%fused_computation.16 | convolution fusion | flops 1425342464 | bytes 14155777 | tf_op jit(solution)/shard_map/dot_general | solution.py:36
  432.2 10.4 %all-to-all-done.7 = bf16[8,12,3584]{2,1,0:T(8,128)(2,1)} async-done(((bf16[8,12,3584]{2,1,0:T(8,128)(2,1)}), bf16[8,12,3584]{2,1,0:T(8,128)(2,1)}, u32[]{:S(2)}, u32[]{:S(2)}) %all-to-all-start.7) | async-done | bytes 688160 | tf_op jit(solution)/shard_map/all_to_all | solution.py:48
  (149 shorter events, 99.3 us)
Async XLA Ops:
  51.0 17.1 %collective-permute-start.2 = (bf16[96,3584]{1,0:T(8,128)(2,1)S(1)}, bf16[96,3584]{1,0:T(8,128)(2,1)S(1)}, u32[]{:S(2)}, u32[]{:S(2)}) collective-permute-start(bf16[96,3584]{1,0:T(8,128)(2,1)S(1)} %all_to_all.53), channel_id=1, source_target_pairs={{0,8},{8,0},{16,24},{24,16},{1,9},{9,1},{17,25},{25,17},{2,10},{10... | collective-permute-start | bytes 2064392 | tf_op jit(solution)/shard_map/ppermute | solution.py:11
  68.3 31.0 %collective-permute-start.3 = (bf16[192,3584]{1,0:T(8,128)(2,1)S(1)}, bf16[192,3584]{1,0:T(8,128)(2,1)}, u32[]{:S(2)}, u32[]{:S(2)}) collective-permute-start(bf16[192,3584]{1,0:T(8,128)(2,1)S(1)} %maximum_select_fusion.5), channel_id=1, source_target_pairs={{0,16},{8,24},{16,0},{24,8},{1,17},{9,25},{17,1},{25,9},{2,18},{10... | collective-permute-start | bytes 4128776 | tf_op jit(solution)/shard_map/ppermute | solution.py:11
  69.9 41.7 %all-to-all-start = ((bf16[8,12,3584]{2,1,0:T(8,128)(2,1)}), bf16[8,12,3584]{2,1,0:T(8,128)(2,1)S(1)}, u32[]{:S(2)}, u32[]{:S(2)}) async-start(bf16[8,12,3584]{2,1,0:T(8,128)(2,1)} %get-tuple-element.36), calls=%async_computation | async-start | bytes 1835008 | tf_op jit(solution)/shard_map/all_to_all | solution.py:42
  73.5 250.6 %reduce-scatter.7.cloned.1.call-start = ((), (), s32[]{:S(2)}) async-start(), calls=%async_computation.13 | async-start | bytes 3440640 | tf_op jit(solution)/shard_map/reduce_scatter | solution.py:47
  111.8 25.4 %collective-permute-start = (bf16[96,3584]{1,0:T(8,128)(2,1)S(1)}, bf16[96,3584]{1,0:T(8,128)(2,1)}, u32[]{:S(2)}, u32[]{:S(2)}) collective-permute-start(bf16[96,3584]{1,0:T(8,128)(2,1)S(1)} %all_to_all.49), channel_id=1, source_target_pairs={{0,8},{8,0},{16,24},{24,16},{1,9},{9,1},{17,25},{25,17},{2,10},{10... | collective-permute-start | bytes 2064392 | tf_op jit(solution)/shard_map/ppermute | solution.py:11
  139.8 33.9 %collective-permute-start.1 = (bf16[192,3584]{1,0:T(8,128)(2,1)}, bf16[192,3584]{1,0:T(8,128)(2,1)}, u32[]{:S(2)}, u32[]{:S(2)}) collective-permute-start(bf16[192,3584]{1,0:T(8,128)(2,1)} %maximum_select_fusion.4), channel_id=1, source_target_pairs={{0,16},{8,24},{16,0},{24,8},{1,17},{9,25},{17,1},{25,9},{2,18},{10... | collective-permute-start | bytes 4128776 | tf_op jit(solution)/shard_map/ppermute | solution.py:11
  143.1 44.6 %all-to-all-start.4 = ((bf16[8,12,3584]{2,1,0:T(8,128)(2,1)}), bf16[8,12,3584]{2,1,0:T(8,128)(2,1)S(1)}, u32[]{:S(2)}, u32[]{:S(2)}) async-start(bf16[8,12,3584]{2,1,0:T(8,128)(2,1)} %get-tuple-element.34), calls=%async_computation.6 | async-start | bytes 1835008 | tf_op jit(solution)/shard_map/all_to_all | solution.py:42
  146.6 197.1 %reduce-scatter.5.cloned.1.call-start = ((), (), s32[]{:S(2)}) async-start(), calls=%async_computation.12 | async-start | bytes 3440640 | tf_op jit(solution)/shard_map/reduce_scatter | solution.py:47
  187.9 17.2 %collective-permute-start.4 = (bf16[96,3584]{1,0:T(8,128)(2,1)S(1)}, bf16[96,3584]{1,0:T(8,128)(2,1)S(1)}, u32[]{:S(2)}, u32[]{:S(2)}) collective-permute-start(bf16[96,3584]{1,0:T(8,128)(2,1)S(1)} %all_to_all.57), channel_id=1, source_target_pairs={{0,8},{8,0},{16,24},{24,16},{1,9},{9,1},{17,25},{25,17},{2,10},{10... | collective-permute-start | bytes 2064392 | tf_op jit(solution)/shard_map/ppermute | solution.py:11
  206.4 40.5 %collective-permute-start.5 = (bf16[192,3584]{1,0:T(8,128)(2,1)}, bf16[192,3584]{1,0:T(8,128)(2,1)}, u32[]{:S(2)}, u32[]{:S(2)}) collective-permute-start(bf16[192,3584]{1,0:T(8,128)(2,1)} %maximum_select_fusion.6), channel_id=1, source_target_pairs={{0,16},{8,24},{16,0},{24,8},{1,17},{9,25},{17,1},{25,9},{2,18},{10... | collective-permute-start | bytes 4128776 | tf_op jit(solution)/shard_map/ppermute | solution.py:11
  206.4 52.2 %all-to-all-start.6 = ((bf16[8,12,3584]{2,1,0:T(8,128)(2,1)}), bf16[8,12,3584]{2,1,0:T(8,128)(2,1)S(1)}, u32[]{:S(2)}, u32[]{:S(2)}) async-start(bf16[8,12,3584]{2,1,0:T(8,128)(2,1)} %get-tuple-element.35), calls=%async_computation.9 | async-start | bytes 1835008 | tf_op jit(solution)/shard_map/all_to_all | solution.py:42
  211.9 168.2 %reduce-scatter.9.cloned.1.call-start = ((), (), s32[]{:S(2)}) async-start(), calls=%async_computation.14 | async-start | bytes 3440640 | tf_op jit(solution)/shard_map/reduce_scatter | solution.py:47
  212.0 40.8 %copy-start = (bf16[1,3584,512]{2,1,0:T(8,128)(2,1)S(1)}, bf16[1,3584,512]{2,1,0:T(8,128)(2,1)}, u32[]{:S(2)}) copy-start(bf16[1,3584,512]{2,1,0:T(8,128)(2,1)} %param.11) | copy-start | bytes 11010052
  258.3 149.0 %reduce-scatter.11.cloned.1.call-start = ((), (), s32[]{:S(2)}) async-start(), calls=%async_computation.15 | async-start | bytes 3440640 | tf_op jit(solution)/shard_map/reduce_scatter | solution.py:47
  258.7 55.5 %copy-start.26 = (f32[384,512]{1,0:T(8,128)S(1)}, f32[384,512]{1,0:T(8,128)}, u32[]{:S(2)}) copy-start(f32[384,512]{1,0:T(8,128)} %copy-done.25) | copy-start | bytes 2359300
  258.7 55.5 %copy-start.28 = (f32[384,512]{1,0:T(8,128)S(1)}, f32[384,512]{1,0:T(8,128)}, u32[]{:S(2)}) copy-start(f32[384,512]{1,0:T(8,128)} %get-tuple-element.18) | copy-start | bytes 2359300
  258.8 14.2 %collective-permute-start.6 = (bf16[96,3584]{1,0:T(8,128)(2,1)S(1)}, bf16[96,3584]{1,0:T(8,128)(2,1)S(1)}, u32[]{:S(2)}, u32[]{:S(2)}) collective-permute-start(bf16[96,3584]{1,0:T(8,128)(2,1)S(1)} %all_to_all.61), channel_id=1, source_target_pairs={{0,8},{8,0},{16,24},{24,16},{1,9},{9,1},{17,25},{25,17},{2,10},{10... | collective-permute-start | bytes 2064392 | tf_op jit(solution)/shard_map/ppermute | solution.py:11
  273.2 45.5 %copy-start.12 = (bf16[192,3584]{1,0:T(8,128)(2,1)}, bf16[192,3584]{1,0:T(8,128)(2,1)S(1)}, u32[]{:S(2)}) copy-start(bf16[192,3584]{1,0:T(8,128)(2,1)S(1)} %maximum_select_fusion.7) | copy-start | bytes 4128772
  273.2 45.5 %copy-start.1 = (bf16[1,3584,512]{2,1,0:T(8,128)(2,1)S(1)}, bf16[1,3584,512]{2,1,0:T(8,128)(2,1)}, u32[]{:S(2)}) copy-start(bf16[1,3584,512]{2,1,0:T(8,128)(2,1)} %param.11) | copy-start | bytes 11010052
  273.2 41.1 %collective-permute-start.7 = (bf16[192,3584]{1,0:T(8,128)(2,1)S(1)}, bf16[192,3584]{1,0:T(8,128)(2,1)S(1)}, u32[]{:S(2)}, u32[]{:S(2)}) collective-permute-start(bf16[192,3584]{1,0:T(8,128)(2,1)S(1)} %maximum_select_fusion.7), channel_id=1, source_target_pairs={{0,16},{8,24},{16,0},{24,8},{1,17},{9,25},{17,1},{25,9},{2,18},{10... | collective-permute-start | bytes 4128776 | tf_op jit(solution)/shard_map/ppermute | solution.py:11
  326.1 33.7 %all-to-all-start.3 = ((bf16[8,12,3584]{2,1,0:T(8,128)(2,1)}), bf16[8,12,3584]{2,1,0:T(8,128)(2,1)S(1)}, u32[]{:S(2)}, u32[]{:S(2)}) async-start(bf16[8,12,3584]{2,1,0:T(8,128)(2,1)} %all_to_all.54), calls=%async_computation.5 | async-start | bytes 1835008 | tf_op jit(solution)/shard_map/all_to_all | solution.py:48
  359.8 27.3 %all-to-all-start.1 = ((bf16[8,12,3584]{2,1,0:T(8,128)(2,1)}), bf16[8,12,3584]{2,1,0:T(8,128)(2,1)S(1)}, u32[]{:S(2)}, u32[]{:S(2)}) async-start(bf16[8,12,3584]{2,1,0:T(8,128)(2,1)} %all_to_all.50), calls=%async_computation.2 | async-start | bytes 1835008 | tf_op jit(solution)/shard_map/all_to_all | solution.py:48
  387.1 27.5 %all-to-all-start.5 = ((bf16[8,12,3584]{2,1,0:T(8,128)(2,1)}), bf16[8,12,3584]{2,1,0:T(8,128)(2,1)S(1)}, u32[]{:S(2)}, u32[]{:S(2)}) async-start(bf16[8,12,3584]{2,1,0:T(8,128)(2,1)} %all_to_all.58), calls=%async_computation.8 | async-start | bytes 1835008 | tf_op jit(solution)/shard_map/all_to_all | solution.py:48
  414.6 28.0 %all-to-all-start.7 = ((bf16[8,12,3584]{2,1,0:T(8,128)(2,1)}), bf16[8,12,3584]{2,1,0:T(8,128)(2,1)}, u32[]{:S(2)}, u32[]{:S(2)}) async-start(bf16[8,12,3584]{2,1,0:T(8,128)(2,1)} %all_to_all.62), calls=%async_computation.11 | async-start | bytes 1835008 | tf_op jit(solution)/shard_map/all_to_all | solution.py:48
  (24 other events, 212.0 us)
Sparse Core Ops, SparseCore 0:
  111.8 55.0 reduce-scatter.6
  187.8 56.0 reduce-scatter.4
  258.5 55.7 reduce-scatter.8
  324.1 45.2 reduce-scatter.10
